TPU v7x, 512 devices: a whole 4x4x16 slice. The times are simulated.
512 devices in a mesh: row: 16 (over z), col: 4 (over x_hi, core), depth: 8 (over y, x_lo).
Axes of the slice: x: 4 (x_hi: 2, x_lo: 2; x = x_hi * 2 + x_lo), y: 4, z: 16, core: 2. Of those that a mesh axis runs over, the one named last changes fastest.
Arguments:
- ks_matrix: bfloat16 [4096, 16384], P('col', ('row', 'depth')), may hold values from -6 to 6
- sign_matrix: bfloat16 [16, 8, 128, 12288], P('col', 'depth', None, 'row'), may hold values from -0.046875 to 0.046875
- ks_mask: int32 [32, 128], P('col', ('row', 'depth')), may hold values 0 or 1
- sign_mask: int32 [16, 8, 1, 96], P('col', 'depth', None, 'row'), may hold values 0 or 1
- product_mask: int32 [32, 96], P('col', 'row'), may hold values 0 or 1
- row_order: int32 [4, 8], P('col'), may hold values from 0 to 7, each once within a row
Outputs:
- next_matrix: bfloat16 [4096, 12288], P(('col', 'depth'), 'row')
Inputs may be any that keep to these rules, and one draw needn't show every extreme that they name: Each row of row_order names every number of 0 to 7 once.
All inputs are finite; a program needn't handle non-finite values. No bound on the sum of `ks_mask` or of `sign_mask` or of `product_mask` on one device may be relied on, other than what follows from the above.
Results may differ from a plain program's by a relative error of at most 0.001.
Values may be sent and summed in bfloat16 or wider, within the bound.
No kernel may reach another device: no remote copies, remote signals or barrier semaphores. Data moves between devices by JAX's collectives and lax.ppermute only.
A program may use at most 64 MiB of HBM per device.

v0:
```python
import jax
import jax.numpy as jnp
from jax import lax
from jax.sharding import PartitionSpec as P

BS = 128


def from_behind(block, axis, distance):
    devices = range(lax.axis_size(axis))
    route = [((i - distance) % len(devices), i) for i in devices]
    return lax.ppermute(block, axis, route)


def per_device(ks_matrix, sign_matrix, ks_mask, sign_mask, product_mask, row_order):
    row_blocks, inner_blocks = ks_mask.shape
    local_groups = sign_mask.shape[0]
    sign_inner = sign_mask.shape[2]
    col_blocks = sign_mask.shape[3]
    ks_panel = (
        ks_matrix.reshape(row_blocks, BS, inner_blocks, BS)
        * ks_mask.astype(jnp.bfloat16)[:, None, :, None]
    )
    ks_panel = ks_panel.reshape(row_blocks * BS, inner_blocks * BS)
    sign_kept = sign_matrix.reshape(local_groups, sign_inner, BS, col_blocks, BS)
    sign_kept = sign_kept * sign_mask.astype(jnp.bfloat16).reshape(
        local_groups, sign_inner, 1, col_blocks, 1
    )
    sign_kept = sign_kept.reshape(local_groups, 1, sign_inner * BS, col_blocks * BS)
    sign_whole = lax.all_gather(sign_kept, "col", axis=0, tiled=True)
    row_count = lax.axis_size("row")
    start_sum = jnp.zeros((row_blocks * BS, col_blocks * BS), jnp.float32)
    row_index = lax.axis_index("row")

    def advance(step, carry):
        running, moving = carry
        source = (row_index - step) % row_count
        sign_piece = lax.dynamic_index_in_dim(sign_whole, source, 0, keepdims=False)[0]
        running = running + jnp.dot(moving, sign_piece, preferred_element_type=jnp.float32)
        moving = from_behind(moving, "row", 1)
        return (running, moving)

    running, moving = lax.fori_loop(0, row_count - 1, advance, (start_sum, ks_panel))
    final_source = (row_index - row_count + 1) % row_count
    final_piece = lax.dynamic_index_in_dim(sign_whole, final_source, 0, keepdims=False)[0]
    running = running + jnp.dot(moving, final_piece, preferred_element_type=jnp.float32)
    depth_count = lax.axis_size("depth")
    part_rows = row_blocks // depth_count
    filtered = (
        running.reshape(row_blocks, BS, col_blocks, BS)
        * product_mask.astype(jnp.float32)[:, None, :, None]
    )
    local_order = row_order[0]
    summed = lax.psum(filtered, "depth")
    own_rows = lax.dynamic_slice_in_dim(
        local_order, lax.axis_index("depth") * part_rows, part_rows, 0
    )
    picked = jnp.take(summed, own_rows, axis=0)
    return picked.reshape(part_rows * BS, col_blocks * BS).astype(jnp.bfloat16)


def solution(mesh):
    in_specs = (
        P("col", ("row", "depth")),
        P("col", "depth", None, "row"),
        P("col", ("row", "depth")),
        P("col", "depth", None, "row"),
        P("col", "row"),
        P("col", None),
    )
    out_specs = P(("col", "depth"), "row")
    return jax.shard_map(
        per_device, mesh=mesh, in_specs=in_specs, out_specs=out_specs, check_vma=False
    )
```

profile of v0, /device:TPU:4, one launch (start us, length us, event | category | flops | bytes accessed | tf_op | source)
XLA Modules:
  0.0 356.8 jit_solution(18374426383536028386)
XLA Ops:
  7.3 2.1 broadcast_multiply_fusion.1
  15.4 36.3 %all-gather.2.cloned.1.call-done = bf16[16,1,128,768]{3,2,1,0:T(8,128)(2,1)} async-done(((bf16[4,1,128,768]{3,2,1,0:T(8,128)(2,1)}), bf16[16,1,128,768]{3,2,1,0:T(8,128)(2,1)}) %all-gather.2.cloned.1.call-update) | async-done | bytes 3145744 | tf_op jit(solution)/shard_map/all_gather | solution.py:30
  51.6 171.1 %while.19 = (s32[]{:T(128)}, f32[1024,768]{0,1:T(8,128)S(1)}, bf16[1024,128]{1,0:T(8,128)(2,1)}, s32[]{:T(128)}, bf16[16,1,128,768]{3,2,1,0:T(8,128)(2,1)}, /*index=5*/s32[]{:T(128)}, s32[]{:T(128)}, s32[]{:T(128)}, s32[]{:T(128)}) while((s32[]{:T(128)}, f32[1024,768]{0,1:T(8,128)S(1)}, bf16[1024,128]{1,0:T(8,128)(2,1)}, ...), condition=%wide.region_1.2_spmd.clone, body=%wide.region_0.1_spmd.clone.sunk | while | flops 202899472 | bytes 8323374 | solution.py:43
  52.6 3.7 %collective-permute-start = (bf16[1024,128]{1,0:T(8,128)(2,1)S(1)}, bf16[1024,128]{1,0:T(8,128)(2,1)}, u32[]{:S(2)}, u32[]{:S(2)}) collective-permute-start(bf16[1024,128]{1,0:T(8,128)(2,1)S(1)} %copy.29), channel_id=1, source_target_pairs={{480,0},{0,32},{32,64},{64,96},{96,128},{128,160},{160,192},{192,2... | collective-permute-start | bytes 786440 | tf_op jit(solution)/shard_map/while/body/eval_jaxpr/ppermute | solution.py:12
  58.2 7.4 %collective-permute-done = bf16[1024,128]{1,0:T(8,128)(2,1)} collective-permute-done((bf16[1024,128]{1,0:T(8,128)(2,1)S(1)}, bf16[1024,128]{1,0:T(8,128)(2,1)}, u32[]{:S(2)}, u32[]{:S(2)}) %collective-permute-start) | collective-permute-done | bytes 262176 | tf_op jit(solution)/shard_map/while/body/eval_jaxpr/ppermute | solution.py:12
  70.3 7.3 %collective-permute-done = bf16[1024,128]{1,0:T(8,128)(2,1)} collective-permute-done((bf16[1024,128]{1,0:T(8,128)(2,1)S(1)}, bf16[1024,128]{1,0:T(8,128)(2,1)}, u32[]{:S(2)}, u32[]{:S(2)}) %collective-permute-start) | collective-permute-done | bytes 262176 | tf_op jit(solution)/shard_map/while/body/eval_jaxpr/ppermute | solution.py:12
  78.6 1.9 collective-permute-start
  82.4 6.5 %collective-permute-done = bf16[1024,128]{1,0:T(8,128)(2,1)} collective-permute-done((bf16[1024,128]{1,0:T(8,128)(2,1)S(1)}, bf16[1024,128]{1,0:T(8,128)(2,1)}, u32[]{:S(2)}, u32[]{:S(2)}) %collective-permute-start) | collective-permute-done | bytes 262176 | tf_op jit(solution)/shard_map/while/body/eval_jaxpr/ppermute | solution.py:12
  89.9 1.9 collective-permute-start
  93.7 5.7 %collective-permute-done = bf16[1024,128]{1,0:T(8,128)(2,1)} collective-permute-done((bf16[1024,128]{1,0:T(8,128)(2,1)S(1)}, bf16[1024,128]{1,0:T(8,128)(2,1)}, u32[]{:S(2)}, u32[]{:S(2)}) %collective-permute-start) | collective-permute-done | bytes 262176 | tf_op jit(solution)/shard_map/while/body/eval_jaxpr/ppermute | solution.py:12
  104.2 5.7 %collective-permute-done = bf16[1024,128]{1,0:T(8,128)(2,1)} collective-permute-done((bf16[1024,128]{1,0:T(8,128)(2,1)S(1)}, bf16[1024,128]{1,0:T(8,128)(2,1)}, u32[]{:S(2)}, u32[]{:S(2)}) %collective-permute-start) | collective-permute-done | bytes 262176 | tf_op jit(solution)/shard_map/while/body/eval_jaxpr/ppermute | solution.py:12
  110.9 1.9 collective-permute-start
  114.7 5.7 %collective-permute-done = bf16[1024,128]{1,0:T(8,128)(2,1)} collective-permute-done((bf16[1024,128]{1,0:T(8,128)(2,1)S(1)}, bf16[1024,128]{1,0:T(8,128)(2,1)}, u32[]{:S(2)}, u32[]{:S(2)}) %collective-permute-start) | collective-permute-done | bytes 262176 | tf_op jit(solution)/shard_map/while/body/eval_jaxpr/ppermute | solution.py:12
  121.4 1.9 collective-permute-start
  125.2 5.7 %collective-permute-done = bf16[1024,128]{1,0:T(8,128)(2,1)} collective-permute-done((bf16[1024,128]{1,0:T(8,128)(2,1)S(1)}, bf16[1024,128]{1,0:T(8,128)(2,1)}, u32[]{:S(2)}, u32[]{:S(2)}) %collective-permute-start) | collective-permute-done | bytes 262176 | tf_op jit(solution)/shard_map/while/body/eval_jaxpr/ppermute | solution.py:12
  135.8 6.7 %collective-permute-done = bf16[1024,128]{1,0:T(8,128)(2,1)} collective-permute-done((bf16[1024,128]{1,0:T(8,128)(2,1)S(1)}, bf16[1024,128]{1,0:T(8,128)(2,1)}, u32[]{:S(2)}, u32[]{:S(2)}) %collective-permute-start) | collective-permute-done | bytes 262176 | tf_op jit(solution)/shard_map/while/body/eval_jaxpr/ppermute | solution.py:12
  147.3 7.9 %collective-permute-done = bf16[1024,128]{1,0:T(8,128)(2,1)} collective-permute-done((bf16[1024,128]{1,0:T(8,128)(2,1)S(1)}, bf16[1024,128]{1,0:T(8,128)(2,1)}, u32[]{:S(2)}, u32[]{:S(2)}) %collective-permute-start) | collective-permute-done | bytes 262176 | tf_op jit(solution)/shard_map/while/body/eval_jaxpr/ppermute | solution.py:12
  156.2 1.9 collective-permute-start
  160.0 8.0 %collective-permute-done = bf16[1024,128]{1,0:T(8,128)(2,1)} collective-permute-done((bf16[1024,128]{1,0:T(8,128)(2,1)S(1)}, bf16[1024,128]{1,0:T(8,128)(2,1)}, u32[]{:S(2)}, u32[]{:S(2)}) %collective-permute-start) | collective-permute-done | bytes 262176 | tf_op jit(solution)/shard_map/while/body/eval_jaxpr/ppermute | solution.py:12
  169.0 1.9 collective-permute-start
  172.8 7.2 %collective-permute-done = bf16[1024,128]{1,0:T(8,128)(2,1)} collective-permute-done((bf16[1024,128]{1,0:T(8,128)(2,1)S(1)}, bf16[1024,128]{1,0:T(8,128)(2,1)}, u32[]{:S(2)}, u32[]{:S(2)}) %collective-permute-start) | collective-permute-done | bytes 262176 | tf_op jit(solution)/shard_map/while/body/eval_jaxpr/ppermute | solution.py:12
  181.0 1.9 collective-permute-start
  184.8 6.3 %collective-permute-done = bf16[1024,128]{1,0:T(8,128)(2,1)} collective-permute-done((bf16[1024,128]{1,0:T(8,128)(2,1)S(1)}, bf16[1024,128]{1,0:T(8,128)(2,1)}, u32[]{:S(2)}, u32[]{:S(2)}) %collective-permute-start) | collective-permute-done | bytes 262176 | tf_op jit(solution)/shard_map/while/body/eval_jaxpr/ppermute | solution.py:12
  195.9 5.7 %collective-permute-done = bf16[1024,128]{1,0:T(8,128)(2,1)} collective-permute-done((bf16[1024,128]{1,0:T(8,128)(2,1)S(1)}, bf16[1024,128]{1,0:T(8,128)(2,1)}, u32[]{:S(2)}, u32[]{:S(2)}) %collective-permute-start) | collective-permute-done | bytes 262176 | tf_op jit(solution)/shard_map/while/body/eval_jaxpr/ppermute | solution.py:12
  206.4 5.7 %collective-permute-done = bf16[1024,128]{1,0:T(8,128)(2,1)} collective-permute-done((bf16[1024,128]{1,0:T(8,128)(2,1)S(1)}, bf16[1024,128]{1,0:T(8,128)(2,1)}, u32[]{:S(2)}, u32[]{:S(2)}) %collective-permute-start) | collective-permute-done | bytes 262176 | tf_op jit(solution)/shard_map/while/body/eval_jaxpr/ppermute | solution.py:12
  217.0 5.7 %collective-permute-done = bf16[1024,128]{1,0:T(8,128)(2,1)} collective-permute-done((bf16[1024,128]{1,0:T(8,128)(2,1)S(1)}, bf16[1024,128]{1,0:T(8,128)(2,1)}, u32[]{:S(2)}, u32[]{:S(2)}) %collective-permute-start) | collective-permute-done | bytes 262176 | tf_op jit(solution)/shard_map/while/body/eval_jaxpr/ppermute | solution.py:12
  222.7 2.4 copy.12
  225.1 2.6 convolution_add_fusion
  227.7 2.3 copy.13
  230.0 2.6 copy.19
  233.0 114.2 %all-reduce.1 = bf16[8,128,6,128]{1,0,3,2:T(8,128)(2,1)} all-reduce(f32[8,128,6,128]{1,0,3,2:T(8,128)S(1)} %broadcast_multiply_fusion), channel_id=1, replica_groups=mesh['row'=16,'col'=4,'depth'=8] {'depth'}, use_global_device_ids=true, to_apply=%region_2.3 | all-reduce | flops 786432 | bytes 4718592 | tf_op jit(solution)/shard_map/psum | solution.py:54
  347.1 1.9 fusion.3
  (55 shorter events, 61.6 us)
Async XLA Ops:
  6.5 3.7 %copy-start = (s32[1,8]{1,0:T(1,128)S(1)}, s32[1,8]{1,0:T(1,128)}, u32[]{:S(2)}) copy-start(s32[1,8]{1,0:T(1,128)} %param.13) | copy-start | bytes 100
  6.5 45.1 %all-gather.2.cloned.1.call-start = ((), (), s32[]{:S(2)}) async-start(), calls=%async_computation | async-start | bytes 3932160 | tf_op jit(solution)/shard_map/all_gather | solution.py:30
  52.6 13.0 %collective-permute-start = (bf16[1024,128]{1,0:T(8,128)(2,1)S(1)}, bf16[1024,128]{1,0:T(8,128)(2,1)}, u32[]{:S(2)}, u32[]{:S(2)}) collective-permute-start(bf16[1024,128]{1,0:T(8,128)(2,1)S(1)} %copy.29), channel_id=1, source_target_pairs={{480,0},{0,32},{32,64},{64,96},{96,128},{128,160},{160,192},{192,2... | collective-permute-start | bytes 786440 | tf_op jit(solution)/shard_map/while/body/eval_jaxpr/ppermute | solution.py:12
  66.5 11.2 %collective-permute-start = (bf16[1024,128]{1,0:T(8,128)(2,1)S(1)}, bf16[1024,128]{1,0:T(8,128)(2,1)}, u32[]{:S(2)}, u32[]{:S(2)}) collective-permute-start(bf16[1024,128]{1,0:T(8,128)(2,1)S(1)} %copy.29), channel_id=1, source_target_pairs={{480,0},{0,32},{32,64},{64,96},{96,128},{128,160},{160,192},{192,2... | collective-permute-start | bytes 786440 | tf_op jit(solution)/shard_map/while/body/eval_jaxpr/ppermute | solution.py:12
  78.6 10.3 %collective-permute-start = (bf16[1024,128]{1,0:T(8,128)(2,1)S(1)}, bf16[1024,128]{1,0:T(8,128)(2,1)}, u32[]{:S(2)}, u32[]{:S(2)}) collective-permute-start(bf16[1024,128]{1,0:T(8,128)(2,1)S(1)} %copy.29), channel_id=1, source_target_pairs={{480,0},{0,32},{32,64},{64,96},{96,128},{128,160},{160,192},{192,2... | collective-permute-start | bytes 786440 | tf_op jit(solution)/shard_map/while/body/eval_jaxpr/ppermute | solution.py:12
  89.9 9.6 %collective-permute-start = (bf16[1024,128]{1,0:T(8,128)(2,1)S(1)}, bf16[1024,128]{1,0:T(8,128)(2,1)}, u32[]{:S(2)}, u32[]{:S(2)}) collective-permute-start(bf16[1024,128]{1,0:T(8,128)(2,1)S(1)} %copy.29), channel_id=1, source_target_pairs={{480,0},{0,32},{32,64},{64,96},{96,128},{128,160},{160,192},{192,2... | collective-permute-start | bytes 786440 | tf_op jit(solution)/shard_map/while/body/eval_jaxpr/ppermute | solution.py:12
  100.4 9.6 %collective-permute-start = (bf16[1024,128]{1,0:T(8,128)(2,1)S(1)}, bf16[1024,128]{1,0:T(8,128)(2,1)}, u32[]{:S(2)}, u32[]{:S(2)}) collective-permute-start(bf16[1024,128]{1,0:T(8,128)(2,1)S(1)} %copy.29), channel_id=1, source_target_pairs={{480,0},{0,32},{32,64},{64,96},{96,128},{128,160},{160,192},{192,2... | collective-permute-start | bytes 786440 | tf_op jit(solution)/shard_map/while/body/eval_jaxpr/ppermute | solution.py:12
  110.9 9.6 %collective-permute-start = (bf16[1024,128]{1,0:T(8,128)(2,1)S(1)}, bf16[1024,128]{1,0:T(8,128)(2,1)}, u32[]{:S(2)}, u32[]{:S(2)}) collective-permute-start(bf16[1024,128]{1,0:T(8,128)(2,1)S(1)} %copy.29), channel_id=1, source_target_pairs={{480,0},{0,32},{32,64},{64,96},{96,128},{128,160},{160,192},{192,2... | collective-permute-start | bytes 786440 | tf_op jit(solution)/shard_map/while/body/eval_jaxpr/ppermute | solution.py:12
  121.4 9.6 %collective-permute-start = (bf16[1024,128]{1,0:T(8,128)(2,1)S(1)}, bf16[1024,128]{1,0:T(8,128)(2,1)}, u32[]{:S(2)}, u32[]{:S(2)}) collective-permute-start(bf16[1024,128]{1,0:T(8,128)(2,1)S(1)} %copy.29), channel_id=1, source_target_pairs={{480,0},{0,32},{32,64},{64,96},{96,128},{128,160},{160,192},{192,2... | collective-permute-start | bytes 786440 | tf_op jit(solution)/shard_map/while/body/eval_jaxpr/ppermute | solution.py:12
  131.9 10.6 %collective-permute-start = (bf16[1024,128]{1,0:T(8,128)(2,1)S(1)}, bf16[1024,128]{1,0:T(8,128)(2,1)}, u32[]{:S(2)}, u32[]{:S(2)}) collective-permute-start(bf16[1024,128]{1,0:T(8,128)(2,1)S(1)} %copy.29), channel_id=1, source_target_pairs={{480,0},{0,32},{32,64},{64,96},{96,128},{128,160},{160,192},{192,2... | collective-permute-start | bytes 786440 | tf_op jit(solution)/shard_map/while/body/eval_jaxpr/ppermute | solution.py:12
  143.5 11.8 %collective-permute-start = (bf16[1024,128]{1,0:T(8,128)(2,1)S(1)}, bf16[1024,128]{1,0:T(8,128)(2,1)}, u32[]{:S(2)}, u32[]{:S(2)}) collective-permute-start(bf16[1024,128]{1,0:T(8,128)(2,1)S(1)} %copy.29), channel_id=1, source_target_pairs={{480,0},{0,32},{32,64},{64,96},{96,128},{128,160},{160,192},{192,2... | collective-permute-start | bytes 786440 | tf_op jit(solution)/shard_map/while/body/eval_jaxpr/ppermute | solution.py:12
  156.2 11.8 %collective-permute-start = (bf16[1024,128]{1,0:T(8,128)(2,1)S(1)}, bf16[1024,128]{1,0:T(8,128)(2,1)}, u32[]{:S(2)}, u32[]{:S(2)}) collective-permute-start(bf16[1024,128]{1,0:T(8,128)(2,1)S(1)} %copy.29), channel_id=1, source_target_pairs={{480,0},{0,32},{32,64},{64,96},{96,128},{128,160},{160,192},{192,2... | collective-permute-start | bytes 786440 | tf_op jit(solution)/shard_map/while/body/eval_jaxpr/ppermute | solution.py:12
  169.0 11.1 %collective-permute-start = (bf16[1024,128]{1,0:T(8,128)(2,1)S(1)}, bf16[1024,128]{1,0:T(8,128)(2,1)}, u32[]{:S(2)}, u32[]{:S(2)}) collective-permute-start(bf16[1024,128]{1,0:T(8,128)(2,1)S(1)} %copy.29), channel_id=1, source_target_pairs={{480,0},{0,32},{32,64},{64,96},{96,128},{128,160},{160,192},{192,2... | collective-permute-start | bytes 786440 | tf_op jit(solution)/shard_map/while/body/eval_jaxpr/ppermute | solution.py:12
  181.0 10.2 %collective-permute-start = (bf16[1024,128]{1,0:T(8,128)(2,1)S(1)}, bf16[1024,128]{1,0:T(8,128)(2,1)}, u32[]{:S(2)}, u32[]{:S(2)}) collective-permute-start(bf16[1024,128]{1,0:T(8,128)(2,1)S(1)} %copy.29), channel_id=1, source_target_pairs={{480,0},{0,32},{32,64},{64,96},{96,128},{128,160},{160,192},{192,2... | collective-permute-start | bytes 786440 | tf_op jit(solution)/shard_map/while/body/eval_jaxpr/ppermute | solution.py:12
  192.1 9.6 %collective-permute-start = (bf16[1024,128]{1,0:T(8,128)(2,1)S(1)}, bf16[1024,128]{1,0:T(8,128)(2,1)}, u32[]{:S(2)}, u32[]{:S(2)}) collective-permute-start(bf16[1024,128]{1,0:T(8,128)(2,1)S(1)} %copy.29), channel_id=1, source_target_pairs={{480,0},{0,32},{32,64},{64,96},{96,128},{128,160},{160,192},{192,2... | collective-permute-start | bytes 786440 | tf_op jit(solution)/shard_map/while/body/eval_jaxpr/ppermute | solution.py:12
  202.6 9.6 %collective-permute-start = (bf16[1024,128]{1,0:T(8,128)(2,1)S(1)}, bf16[1024,128]{1,0:T(8,128)(2,1)}, u32[]{:S(2)}, u32[]{:S(2)}) collective-permute-start(bf16[1024,128]{1,0:T(8,128)(2,1)S(1)} %copy.29), channel_id=1, source_target_pairs={{480,0},{0,32},{32,64},{64,96},{96,128},{128,160},{160,192},{192,2... | collective-permute-start | bytes 786440 | tf_op jit(solution)/shard_map/while/body/eval_jaxpr/ppermute | solution.py:12
  213.1 9.6 %collective-permute-start = (bf16[1024,128]{1,0:T(8,128)(2,1)S(1)}, bf16[1024,128]{1,0:T(8,128)(2,1)}, u32[]{:S(2)}, u32[]{:S(2)}) collective-permute-start(bf16[1024,128]{1,0:T(8,128)(2,1)S(1)} %copy.29), channel_id=1, source_target_pairs={{480,0},{0,32},{32,64},{64,96},{96,128},{128,160},{160,192},{192,2... | collective-permute-start | bytes 786440 | tf_op jit(solution)/shard_map/while/body/eval_jaxpr/ppermute | solution.py:12
Sparse Core Ops, SparseCore 0:
  9.5 42.0 all-gather.1
where the time goes:
time: 358 us; the launch traced here: 357 us
  waiting for transfers between devices  134 us (37%)
  blocking collectives  114 us (32%)
  matrix products  30.7 us (9%)
  starting transfers between devices  30.4 us (8%)
  local copies, waits for them, and re-layouts  23.3 us (7%)
  between operations  15.4 us (4%)
  other arithmetic  8.19 us (2%)
    psum x1, blocking collectives, per_device(): summed = lax.psum(filtered, 'depth')  114 us
    ppermute x15, waiting for transfers between devices, from_behind(): return lax.ppermute(block, axis, route)  97.7 us
    all_gather x1, waiting for transfers between devices, per_device(): sign_whole = lax.all_gather(sign_kept, 'col', axis=0, tiled=True)  36.3 us
    ppermute x15, starting transfers between devices, from_behind(): return lax.ppermute(block, axis, route)  30.4 us
    dot_general x15, matrix products, advance(): jnp.dot(moving, sign_piece, preferred_element_type=jnp.float32)  28.1 us
    while x15, local copies, waits for them, and re-layouts  14.3 us
  transfers between devices with their start and end apart: 16, of which 16 were waited for; matrix products, arithmetic and copies ran while one was open for 9% of the time, Pallas kernels for 0%

commit v1 on v0

--- a/solution.py
+++ b/solution.py
@@ -4,6 +4,11 @@
 from jax.sharding import PartitionSpec as P
 
 BS = 128
+
+
+def summed_here(value, axis):
+    terms = lax.all_gather(value, axis)
+    return jnp.sum(terms, axis=0)
 
 
 def from_behind(block, axis, distance):
@@ -51,7 +56,7 @@
         * product_mask.astype(jnp.float32)[:, None, :, None]
     )
     local_order = row_order[0]
-    summed = lax.psum(filtered, "depth")
+    summed = summed_here(filtered, "depth")
     own_rows = lax.dynamic_slice_in_dim(
         local_order, lax.axis_index("depth") * part_rows, part_rows, 0
     )

time: 358 us -> 747 us (2.09)
  the two profiles are of different devices: /device:TPU:4 before, /device:TPU:1 now
where the time goes in v1:
time: 747 us; the launch traced here: 745 us
  waiting for transfers between devices  626 us (84%)
  matrix products  30.7 us (4%)
  starting transfers between devices  29.9 us (4%)
  local copies, waits for them, and re-layouts  26.2 us (4%)
  other arithmetic  16.3 us (2%)
  between operations  15.5 us (2%)
    all_gather x1, waiting for transfers between devices, summed_here(): terms = lax.all_gather(value, axis)  501 us
    ppermute x15, waiting for transfers between devices, from_behind(): return lax.ppermute(block, axis, route)  82.7 us
    all_gather x1, waiting for transfers between devices, per_device(): sign_whole = lax.all_gather(sign_kept, 'col', axis=0, tiled=True)  42.7 us
    ppermute x15, starting transfers between devices, from_behind(): return lax.ppermute(block, axis, route)  29.9 us
    dot_general x15, matrix products, advance(): jnp.dot(moving, sign_piece, preferred_element_type=jnp.float32)  28.1 us
  transfers between devices with their start and end apart: 17, of which 17 were waited for; matrix products, arithmetic and copies ran while one was open for 4% of the time, Pallas kernels for 0%

profile of v1, /device:TPU:1, one launch (start us, length us, event | category | flops | bytes accessed | tf_op | source)
XLA Modules:
  0.0 745.1 jit_solution(13880398359097400717)
XLA Ops:
  7.3 2.1 broadcast_multiply_fusion.1
  12.9 42.7 %all-gather.3.cloned.1.call-done = bf16[16,1,128,768]{3,2,1,0:T(8,128)(2,1)} async-done(((bf16[4,1,128,768]{3,2,1,0:T(8,128)(2,1)}), bf16[16,1,128,768]{3,2,1,0:T(8,128)(2,1)}) %all-gather.3.cloned.1.call-update) | async-done | bytes 3145744 | tf_op jit(solution)/shard_map/all_gather | solution.py:35
  55.5 155.6 %while.19 = (s32[]{:T(128)}, f32[1024,768]{0,1:T(8,128)S(1)}, bf16[1024,128]{1,0:T(8,128)(2,1)}, s32[]{:T(128)}, bf16[16,1,128,768]{3,2,1,0:T(8,128)(2,1)}, /*index=5*/s32[]{:T(128)}, s32[]{:T(128)}, s32[]{:T(128)}, s32[]{:T(128)}) while((s32[]{:T(128)}, f32[1024,768]{0,1:T(8,128)S(1)}, bf16[1024,128]{1,0:T(8,128)(2,1)}, ...), condition=%wide.region_1.2_spmd.clone, body=%wide.region_0.1_spmd.clone.sunk | while | flops 202899472 | bytes 8323374 | solution.py:48
  56.5 3.2 collective-permute-start
  61.6 7.2 collective-permute-done
  73.5 6.4 collective-permute-done
  80.9 1.9 collective-permute-start
  84.8 5.5 collective-permute-done
  91.2 1.9 collective-permute-start
  95.1 4.6 collective-permute-done
  100.6 1.9 collective-permute-start
  104.4 4.6 collective-permute-done
  113.8 4.6 collective-permute-done
  119.3 1.9 collective-permute-start
  123.2 4.6 collective-permute-done
  132.5 4.6 collective-permute-done
  138.1 1.9 collective-permute-start
  141.9 5.7 collective-permute-done
  148.5 1.9 collective-permute-start
  152.3 6.7 collective-permute-done
  163.9 7.2 collective-permute-done
  175.9 6.3 collective-permute-done
  187.0 5.4 collective-permute-done
  197.2 4.6 collective-permute-done
  206.5 4.6 collective-permute-done
  211.1 2.4 copy.12
  213.5 2.6 convolution_add_fusion
  216.2 2.4 copy.13
  218.5 2.6 copy.23
  221.5 2.4 copy.15
  226.5 500.5 %all-gather.5.cloned.1.call-done = f32[8,8,128,6,128]{4,2,3,1,0:T(8,128)} async-done(((f32[1,8,128,6,128]{4,2,3,1,0:T(8,128)}), f32[8,8,128,6,128]{4,2,3,1,0:T(8,128)}) %all-gather.5.cloned.1.call-update) | async-done | bytes 25165840 | tf_op jit(solution)/shard_map/all_gather | solution.py:10
  727.0 9.6 %reduce_sum.9 = bf16[8,128,6,128]{3,1,2,0:T(8,128)(2,1)S(1)} reduce(f32[8,8,128,6,128]{4,2,3,1,0:T(8,128)} %all-gather.5.cloned.1.call-done, f32[]{:T(128)} %constant.92.clone.1), dimensions={0}, to_apply=%region_2.3 | reduce | flops 5505024 | bytes 26738692 | tf_op jit(solution)/shard_map/reduce_sum | solution.py:11
  (61 shorter events, 64.4 us)
Async XLA Ops:
  6.5 217.4 %copy-start = (s32[1,8]{1,0:T(1,128)S(1)}, s32[1,8]{1,0:T(1,128)}, u32[]{:S(2)}) copy-start(s32[1,8]{1,0:T(1,128)} %param.13) | copy-start | bytes 100
  6.5 49.0 %all-gather.3.cloned.1.call-start = ((), (), s32[]{:S(2)}) async-start(), calls=%async_computation | async-start | bytes 3932160 | tf_op jit(solution)/shard_map/all_gather | solution.py:35
  9.4 717.5 %all-gather.5.cloned.1.call-start = ((), (), s32[]{:S(2)}) async-start(), calls=%async_computation.1 | async-start | bytes 28311552 | tf_op jit(solution)/shard_map/all_gather | solution.py:10
  56.5 12.3 %collective-permute-start = (bf16[1024,128]{1,0:T(8,128)(2,1)S(1)}, bf16[1024,128]{1,0:T(8,128)(2,1)}, u32[]{:S(2)}, u32[]{:S(2)}) collective-permute-start(bf16[1024,128]{1,0:T(8,128)(2,1)S(1)} %copy.33), channel_id=1, source_target_pairs={{480,0},{0,32},{32,64},{64,96},{96,128},{128,160},{160,192},{192,2... | collective-permute-start | bytes 786440 | tf_op jit(solution)/shard_map/while/body/eval_jaxpr/ppermute | solution.py:17
  69.7 10.3 %collective-permute-start = (bf16[1024,128]{1,0:T(8,128)(2,1)S(1)}, bf16[1024,128]{1,0:T(8,128)(2,1)}, u32[]{:S(2)}, u32[]{:S(2)}) collective-permute-start(bf16[1024,128]{1,0:T(8,128)(2,1)S(1)} %copy.33), channel_id=1, source_target_pairs={{480,0},{0,32},{32,64},{64,96},{96,128},{128,160},{160,192},{192,2... | collective-permute-start | bytes 786440 | tf_op jit(solution)/shard_map/while/body/eval_jaxpr/ppermute | solution.py:17
  80.9 9.4 %collective-permute-start = (bf16[1024,128]{1,0:T(8,128)(2,1)S(1)}, bf16[1024,128]{1,0:T(8,128)(2,1)}, u32[]{:S(2)}, u32[]{:S(2)}) collective-permute-start(bf16[1024,128]{1,0:T(8,128)(2,1)S(1)} %copy.33), channel_id=1, source_target_pairs={{480,0},{0,32},{32,64},{64,96},{96,128},{128,160},{160,192},{192,2... | collective-permute-start | bytes 786440 | tf_op jit(solution)/shard_map/while/body/eval_jaxpr/ppermute | solution.py:17
  91.2 8.4 %collective-permute-start = (bf16[1024,128]{1,0:T(8,128)(2,1)S(1)}, bf16[1024,128]{1,0:T(8,128)(2,1)}, u32[]{:S(2)}, u32[]{:S(2)}) collective-permute-start(bf16[1024,128]{1,0:T(8,128)(2,1)S(1)} %copy.33), channel_id=1, source_target_pairs={{480,0},{0,32},{32,64},{64,96},{96,128},{128,160},{160,192},{192,2... | collective-permute-start | bytes 786440 | tf_op jit(solution)/shard_map/while/body/eval_jaxpr/ppermute | solution.py:17
  100.6 8.4 %collective-permute-start = (bf16[1024,128]{1,0:T(8,128)(2,1)S(1)}, bf16[1024,128]{1,0:T(8,128)(2,1)}, u32[]{:S(2)}, u32[]{:S(2)}) collective-permute-start(bf16[1024,128]{1,0:T(8,128)(2,1)S(1)} %copy.33), channel_id=1, source_target_pairs={{480,0},{0,32},{32,64},{64,96},{96,128},{128,160},{160,192},{192,2... | collective-permute-start | bytes 786440 | tf_op jit(solution)/shard_map/while/body/eval_jaxpr/ppermute | solution.py:17
  110.0 8.4 %collective-permute-start = (bf16[1024,128]{1,0:T(8,128)(2,1)S(1)}, bf16[1024,128]{1,0:T(8,128)(2,1)}, u32[]{:S(2)}, u32[]{:S(2)}) collective-permute-start(bf16[1024,128]{1,0:T(8,128)(2,1)S(1)} %copy.33), channel_id=1, source_target_pairs={{480,0},{0,32},{32,64},{64,96},{96,128},{128,160},{160,192},{192,2... | collective-permute-start | bytes 786440 | tf_op jit(solution)/shard_map/while/body/eval_jaxpr/ppermute | solution.py:17
  119.3 8.4 %collective-permute-start = (bf16[1024,128]{1,0:T(8,128)(2,1)S(1)}, bf16[1024,128]{1,0:T(8,128)(2,1)}, u32[]{:S(2)}, u32[]{:S(2)}) collective-permute-start(bf16[1024,128]{1,0:T(8,128)(2,1)S(1)} %copy.33), channel_id=1, source_target_pairs={{480,0},{0,32},{32,64},{64,96},{96,128},{128,160},{160,192},{192,2... | collective-permute-start | bytes 786440 | tf_op jit(solution)/shard_map/while/body/eval_jaxpr/ppermute | solution.py:17
  128.7 8.4 %collective-permute-start = (bf16[1024,128]{1,0:T(8,128)(2,1)S(1)}, bf16[1024,128]{1,0:T(8,128)(2,1)}, u32[]{:S(2)}, u32[]{:S(2)}) collective-permute-start(bf16[1024,128]{1,0:T(8,128)(2,1)S(1)} %copy.33), channel_id=1, source_target_pairs={{480,0},{0,32},{32,64},{64,96},{96,128},{128,160},{160,192},{192,2... | collective-permute-start | bytes 786440 | tf_op jit(solution)/shard_map/while/body/eval_jaxpr/ppermute | solution.py:17
  138.1 9.5 %collective-permute-start = (bf16[1024,128]{1,0:T(8,128)(2,1)S(1)}, bf16[1024,128]{1,0:T(8,128)(2,1)}, u32[]{:S(2)}, u32[]{:S(2)}) collective-permute-start(bf16[1024,128]{1,0:T(8,128)(2,1)S(1)} %copy.33), channel_id=1, source_target_pairs={{480,0},{0,32},{32,64},{64,96},{96,128},{128,160},{160,192},{192,2... | collective-permute-start | bytes 786440 | tf_op jit(solution)/shard_map/while/body/eval_jaxpr/ppermute | solution.py:17
  148.5 10.6 %collective-permute-start = (bf16[1024,128]{1,0:T(8,128)(2,1)S(1)}, bf16[1024,128]{1,0:T(8,128)(2,1)}, u32[]{:S(2)}, u32[]{:S(2)}) collective-permute-start(bf16[1024,128]{1,0:T(8,128)(2,1)S(1)} %copy.33), channel_id=1, source_target_pairs={{480,0},{0,32},{32,64},{64,96},{96,128},{128,160},{160,192},{192,2... | collective-permute-start | bytes 786440 | tf_op jit(solution)/shard_map/while/body/eval_jaxpr/ppermute | solution.py:17
  160.0 11.1 %collective-permute-start = (bf16[1024,128]{1,0:T(8,128)(2,1)S(1)}, bf16[1024,128]{1,0:T(8,128)(2,1)}, u32[]{:S(2)}, u32[]{:S(2)}) collective-permute-start(bf16[1024,128]{1,0:T(8,128)(2,1)S(1)} %copy.33), channel_id=1, source_target_pairs={{480,0},{0,32},{32,64},{64,96},{96,128},{128,160},{160,192},{192,2... | collective-permute-start | bytes 786440 | tf_op jit(solution)/shard_map/while/body/eval_jaxpr/ppermute | solution.py:17
  172.1 10.2 %collective-permute-start = (bf16[1024,128]{1,0:T(8,128)(2,1)S(1)}, bf16[1024,128]{1,0:T(8,128)(2,1)}, u32[]{:S(2)}, u32[]{:S(2)}) collective-permute-start(bf16[1024,128]{1,0:T(8,128)(2,1)S(1)} %copy.33), channel_id=1, source_target_pairs={{480,0},{0,32},{32,64},{64,96},{96,128},{128,160},{160,192},{192,2... | collective-permute-start | bytes 786440 | tf_op jit(solution)/shard_map/while/body/eval_jaxpr/ppermute | solution.py:17
  183.2 9.2 %collective-permute-start = (bf16[1024,128]{1,0:T(8,128)(2,1)S(1)}, bf16[1024,128]{1,0:T(8,128)(2,1)}, u32[]{:S(2)}, u32[]{:S(2)}) collective-permute-start(bf16[1024,128]{1,0:T(8,128)(2,1)S(1)} %copy.33), channel_id=1, source_target_pairs={{480,0},{0,32},{32,64},{64,96},{96,128},{128,160},{160,192},{192,2... | collective-permute-start | bytes 786440 | tf_op jit(solution)/shard_map/while/body/eval_jaxpr/ppermute | solution.py:17
  193.3 8.4 %collective-permute-start = (bf16[1024,128]{1,0:T(8,128)(2,1)S(1)}, bf16[1024,128]{1,0:T(8,128)(2,1)}, u32[]{:S(2)}, u32[]{:S(2)}) collective-permute-start(bf16[1024,128]{1,0:T(8,128)(2,1)S(1)} %copy.33), channel_id=1, source_target_pairs={{480,0},{0,32},{32,64},{64,96},{96,128},{128,160},{160,192},{192,2... | collective-permute-start | bytes 786440 | tf_op jit(solution)/shard_map/while/body/eval_jaxpr/ppermute | solution.py:17
  202.7 8.4 %collective-permute-start = (bf16[1024,128]{1,0:T(8,128)(2,1)S(1)}, bf16[1024,128]{1,0:T(8,128)(2,1)}, u32[]{:S(2)}, u32[]{:S(2)}) collective-permute-start(bf16[1024,128]{1,0:T(8,128)(2,1)S(1)} %copy.33), channel_id=1, source_target_pairs={{480,0},{0,32},{32,64},{64,96},{96,128},{128,160},{160,192},{192,2... | collective-permute-start | bytes 786440 | tf_op jit(solution)/shard_map/while/body/eval_jaxpr/ppermute | solution.py:17
Sparse Core Ops, SparseCore 0:
  9.5 45.9 all-gather.2
  224.0 502.8 all-gather.4
